TPU v7x, 256 devices: a whole 4x4x8 slice. The times are simulated.
256 devices in a mesh: query: 8 (over x, core), bank: 32 (over z, y).
Axes of the slice: x: 4, y: 4, z: 8, core: 2. Of those that a mesh axis runs over, the one named last changes fastest.
Arguments:
- queries: bfloat16 [2048, 32, 128], P(('query', 'bank'))
- passages: bfloat16 [8192, 128, 128], P('bank')
- passage_home: int32 [8192], replicated, may hold values from 0 to 8191, as said below
- candidates: int32 [2048, 16], P(('query', 'bank')), may hold values from 0 to 8191, as said below
- positive: int32 [2048], P(('query', 'bank')), may hold values from 0 to 15
Outputs:
- losses: float32 [2048], P(('query', 'bank'))
- query_grads: float32 [2048, 32, 128], P(('query', 'bank'))
Inputs may be any that keep to these rules, and one draw needn't show every extreme that they name: `passage_home`: each passage id has its own storage row; storage row r lies on bank index r // 256. `candidates`: among the 128 list entries of one device's queries (aligned blocks of 8 queries, in order), at most 12 name passages stored on one bank index; in every block some bank index gets exactly 12, and in each group of 32 consecutive blocks it is the same bank index for all of them.
All inputs are finite; a program needn't handle non-finite values.
Results may differ from a plain program's by a relative error of at most 0.0049.
Values may be sent and summed in bfloat16 or wider, within the bound.
No kernel may reach another device: no remote copies, remote signals or barrier semaphores. Data moves between devices by JAX's collectives and lax.ppermute only.
A program may use at most 128 MiB of HBM per device.

v0:
```python
import jax
import jax.numpy as jnp
import numpy as np
from jax import lax
from jax.sharding import Mesh
from jax.sharding import PartitionSpec as P

BANK = ("z", "y")


def soft_terms(scores):
    largest = jnp.max(scores, axis=-1, keepdims=True)
    raised = jnp.exp(scores - largest)
    totals = jnp.sum(raised, axis=-1, keepdims=True)
    maxima = largest[..., 0] + jnp.log(totals[..., 0])
    weights = (raised / totals).astype(jnp.bfloat16)
    return (maxima, weights)


def contrast(similarity, positive):
    largest = jnp.max(similarity, axis=1, keepdims=True)
    raised = jnp.exp(similarity - largest)
    totals = jnp.sum(raised, axis=1, keepdims=True)
    picked = jnp.arange(similarity.shape[1], dtype=jnp.int32)[None, :] == positive[:, None]
    losses = (
        largest[:, 0] + jnp.log(totals[:, 0]) - jnp.sum(jnp.where(picked, similarity, 0.0), axis=1)
    )
    coefficients = (raised / totals - picked.astype(jnp.float32)).astype(jnp.bfloat16)
    return (losses, coefficients)


def split3(value):
    high = lax.reduce_precision(value, exponent_bits=8, mantissa_bits=7)
    rest = value - high
    middle = lax.reduce_precision(rest, exponent_bits=8, mantissa_bits=7)
    low = rest - middle
    return jnp.stack([high, middle, low], axis=-1).astype(jnp.bfloat16)


def join3(pieces):
    pieces = pieces.astype(jnp.float32)
    return pieces[..., 0] + pieces[..., 1] + pieces[..., 2]


def gather_bank(value):
    value = lax.all_gather(value, "y", axis=0, tiled=True)
    return lax.all_gather(value, "z", axis=0, tiled=True)


def body(queries, passages, passage_home, candidates, positive):
    shards = lax.axis_size(BANK)
    me = lax.axis_index(BANK)
    query_rows, query_len, feature_dim = queries.shape
    listed = candidates.shape[1]
    holdings = passages.shape[0]
    entries = query_rows * listed
    capacity = 3 * entries // shards
    width = query_len * feature_dim
    tail = 128
    lists = jnp.concatenate([candidates, positive[:, None]], axis=1)
    group_candidates = gather_bank(lists)[:, :listed]
    group_queries = gather_bank(queries)
    storage = passage_home[group_candidates].reshape(shards, entries)
    mine = storage // holdings == me
    position = jnp.cumsum(mine.astype(jnp.int32), axis=1) - 1
    slot_ids = jnp.arange(capacity, dtype=jnp.int32)
    hit = mine[:, None, :] & (position[:, None, :] == slot_ids[None, :, None])
    entry_ids = jnp.arange(entries, dtype=jnp.int32)
    entry = jnp.sum(jnp.where(hit, entry_ids[None, None, :], 0), axis=2)
    local_slot = jnp.sum(jnp.where(hit, (storage % holdings)[:, None, :], 0), axis=2)
    source = jnp.arange(shards, dtype=jnp.int32)[:, None]
    query_index = (source * query_rows + entry // listed).reshape(-1)
    local_slot = local_slot.reshape(-1)
    passage_tiles = passages[local_slot]
    query_tiles = group_queries[query_index]
    scores = jnp.einsum(
        "sid,sjd->sij", query_tiles, passage_tiles, preferred_element_type=jnp.float32
    )
    maxima, weights = soft_terms(scores)
    token_basis = jnp.einsum(
        "sij,sjd->sid", weights, passage_tiles, preferred_element_type=jnp.float32
    ).astype(jnp.bfloat16)
    slot_similarity = split3(jnp.sum(maxima, axis=1)).reshape(shards, capacity * 3)
    payload = jnp.concatenate(
        [
            token_basis.reshape(shards, capacity * width),
            slot_similarity,
            jnp.zeros((shards, tail - capacity * 3), jnp.bfloat16),
        ],
        axis=1,
    )
    returned = lax.all_to_all(payload, BANK, 0, 0, tiled=True)
    own_storage = passage_home[candidates].reshape(entries)
    holder = own_storage // holdings
    member = holder[:, None] == jnp.arange(shards, dtype=jnp.int32)[None, :]
    member = member.astype(jnp.int32)
    own_position = jnp.sum((jnp.cumsum(member, axis=0) - member) * member, axis=1)
    pieces = returned[:, capacity * width : capacity * width + capacity * 3]
    pieces = pieces.reshape(shards * capacity, 3)
    flat_slot = holder * capacity + own_position
    similarity = join3(pieces[flat_slot]).reshape(query_rows, listed)
    losses, coefficients = contrast(similarity, positive)
    slot_of = flat_slot.reshape(query_rows, listed)
    spread = jnp.arange(shards * capacity, dtype=jnp.int32)[None, None, :] == slot_of[:, :, None]
    spread = jnp.sum(
        jnp.where(spread, coefficients[:, :, None].astype(jnp.float32), 0.0), axis=1
    ).astype(jnp.bfloat16)
    bases = returned[:, : capacity * width].reshape(shards * capacity, width)
    gradient = jnp.einsum("qs,sd->qd", spread, bases, preferred_element_type=jnp.float32)
    return (losses, gradient.reshape(query_rows, query_len, feature_dim))


def solution(mesh):
    rows = mesh.shape["query"]
    bank = mesh.shape["bank"]
    across = 4 if bank % 4 == 0 else 1
    devices = np.asarray(mesh.devices).reshape(rows, bank // across, across)
    split_mesh = Mesh(devices, ("query",) + BANK)
    every = ("query",) + BANK
    return jax.shard_map(
        body,
        mesh=split_mesh,
        in_specs=(P(every, None, None), P(BANK, None, None), P(), P(every, None), P(every)),
        out_specs=(P(every), P(every, None, None)),
        check_vma=False,
    )
```

profile of v0, /device:TPU:2, one launch (start us, length us, event | category | flops | bytes accessed | tf_op | source)
XLA Modules:
  0.0 256.7 jit_solution(14263057151190145409)
XLA Ops:
  7.2 0.0 copy-start
  7.2 0.0 all-gather.3.cloned.1.call-start
  7.2 14.5 %all_gather.12 = bf16[32,32,128]{2,1,0:T(8,128)(2,1)} all-gather(bf16[8,32,128]{2,1,0:T(8,128)(2,1)} %param.5), channel_id=1, replica_groups=mesh['query'=8,'z'=8,'y'=4] {'y'}, dimensions={0}, use_global_device_ids=true | all-gather | bytes 327680 | tf_op jit(solution)/shard_map/all_gather | solution.py:46
  21.7 0.0 all-gather.3.cloned.1.call-update
  21.7 0.7 copy.33
  22.4 0.8 pad_add_fusion
  23.2 12.0 %all_gather.14 = s32[32,17]{1,0:T(8,128)S(1)} all-gather(s32[8,17]{1,0:T(8,128)S(1)} %pad_add_fusion), channel_id=1, replica_groups=mesh['query'=8,'z'=8,'y'=4] {'y'}, dimensions={0}, use_global_device_ids=true | all-gather | bytes 2720 | tf_op jit(solution)/shard_map/all_gather | solution.py:46
  35.2 0.1 copy.34
  35.3 28.2 %all-gather = s32[8,32,17]{1,2,0:T(8,128)S(1)} all-gather(s32[1,32,17]{1,2,0:T(8,128)S(1)} %copy.34), channel_id=1, replica_groups=mesh['query'=8,'z'=8,'y'=4] {'z'}, dimensions={0}, use_global_device_ids=true | all-gather | bytes 19584 | tf_op jit(solution)/shard_map/all_gather | solution.py:47
  63.5 0.1 reshape.533
  63.6 0.1 copy.36
  63.7 0.1 reshape.487
  63.9 23.0 %gather_fusion = s32[4096]{0:T(1024)S(1)} fusion(s32[8192]{0:T(1024)S(1)} %copy-done, s32[4096]{0:T(1024)S(1)} %broadcast_clamp_fusion), kind=kCustom, calls=%fused_computation | custom fusion | bytes 49152 | tf_op jit(solution)/shard_map/gather | solution.py:63
  87.0 0.3 reduce_window_sum.22
  87.3 0.5 select_reduce_fusion.2
  87.7 0.1 copy.38
  87.8 0.1 reshape.479
  88.0 0.1 add.180
  88.0 0.1 add.181
  88.1 0.1 copy.37
  88.2 0.1 reduce_sum.81
  88.4 14.4 %gather_fusion.2 = bf16[384,128,128]{2,1,0:T(8,128)(2,1)} fusion(bf16[256,128,128]{2,1,0:T(8,128)(2,1)} %param.6, s32[1024]{0:T(1024)S(1)} %pad_clamp_fusion.2), kind=kCustom, calls=%fused_computation.2 | custom fusion | bytes 25167360 | tf_op jit(solution)/shard_map/gather | solution.py:74
  102.8 0.0 all-gather.3.cloned.1.call-done
  102.9 2.8 %gather_fusion.1 = bf16[384,32,128]{2,1,0:T(8,128)(2,1)S(1)} fusion(bf16[256,32,128]{2,1,0:T(8,128)(2,1)} %all-gather.3.cloned.1.call-done, s32[1024]{0:T(1024)S(1)} %pad_clamp_fusion.3), kind=kCustom, calls=%fused_computation.1 | custom fusion | bytes 6292992 | tf_op jit(solution)/shard_map/gather | solution.py:75
  105.7 11.3 %fusion.27 = (f32[384,32]{1,0:T(8,128)S(1)}, f32[384,32,128]{2,1,0:T(8,128)}) fusion(bf16[384,32,128]{2,1,0:T(8,128)(2,1)S(1)} %gather_fusion.1, bf16[384,128,128]{2,1,0:T(8,128)(2,1)} %gather_fusion.2), kind=kOutput, calls=%fused_computation.94 | convolution fusion | flops 404213760 | bytes 22069248 | tf_op jit(solution)/shard_map/sid,sjd->sij/dot_general | solution.py:76
  117.0 5.8 %fusion = f32[384,32]{1,0:T(8,128)S(1)} fusion(f32[384,32,128]{2,1,0:T(8,128)} %get-tuple-element.24, f32[384,32]{1,0:T(8,128)S(1)} %get-tuple-element.23), kind=kLoop, calls=%fused_computation.7 | loop fusion | flops 3133440 | bytes 6389760 | tf_op jit(solution)/shard_map/reduce_sum | solution.py:14
  122.9 7.1 %fusion.4 = bf16[384,32,128]{2,1,0:T(8,128)(2,1)S(1)} fusion(bf16[384,128,128]{2,1,0:T(8,128)(2,1)} %gather_fusion.2, f32[384,32,128]{2,1,0:T(8,128)S(1)} %copy-done.1, f32[384,32]{1,0:T(8,128)S(1)} %fusion, f32[384,32]{1,0:T(8,128)S(1)} %get-tuple-element.23), kind=kOutput, calls=%fused_computation.12 | convolution fusion | flops 408944640 | bytes 22118400 | tf_op jit(solution)/shard_map/sij,sjd->sid/dot_general | solution.py:80
  130.0 0.2 add_reduce_fusion
  130.2 2.8 %reshape.480 = bf16[32,49152]{1,0:T(8,128)(2,1)} reshape(bf16[384,32,128]{2,1,0:T(8,128)(2,1)S(1)} %fusion.4) | data formatting | bytes 6291456 | tf_op jit(solution)/shard_map/reshape | solution.py:86
  133.0 2.1 constant_dynamic-update-slice_fusion
  135.1 0.2 copy.39
  135.3 0.1 convert_element_type.52
  135.5 0.2 dynamic-update-slice.1
  135.6 0.3 dynamic-update-slice.2
  136.0 1.7 copy-done.2
  137.6 0.5 broadcast.445
  138.1 5.0 %reduce.6 = bf16[32,49280]{1,0:T(8,128)(2,1)S(1)} reduce(bf16[32,1,49280]{2,0,1:T(8,128)(2,1)} %bitcast.63, bf16[]{:T(256)} %broadcast.445), dimensions={1}, to_apply=%copy.40.reduce_sub_computation | reduce | bytes 6307842 | tf_op jit(solution)/shard_map/all_to_all | solution.py:92
  143.1 3.6 %reshape.538 = bf16[32,2,24640]{2,1,0:T(2,128)(2,1)} reshape(bf16[32,49280]{1,0:T(8,128)(2,1)S(1)} %reduce.6) | data formatting | bytes 6307840
  146.7 6.5 %all-to-all-start = ((bf16[32,2,24640]{2,1,0:T(2,128)(2,1)}), bf16[32,2,24640]{2,1,0:T(2,128)(2,1)S(1)}, u32[]{:S(2)}, u32[]{:S(2)}) async-start(bf16[32,2,24640]{2,1,0:T(2,128)(2,1)} %reshape.538), calls=%async_computation | async-start | bytes 6324224 | tf_op jit(solution)/shard_map/all_to_all | solution.py:92
  153.3 0.1 reshape.511
  153.4 1.1 gather_fusion.3
  154.5 0.1 reshape.510
  154.6 0.1 fusion.7
  154.7 0.2 reduce_window_sum.23
  154.9 0.2 select_reduce_fusion.3
  155.1 0.1 reduce_sum.90
  155.2 62.0 %all-to-all-done = bf16[32,2,24640]{2,1,0:T(2,128)(2,1)S(1)} async-done(((bf16[32,2,24640]{2,1,0:T(2,128)(2,1)}), bf16[32,2,24640]{2,1,0:T(2,128)(2,1)S(1)}, u32[]{:S(2)}, u32[]{:S(2)}) %all-to-all-start) | async-done | bytes 3153952 | tf_op jit(solution)/shard_map/all_to_all | solution.py:92
  217.2 16.4 %reshape.539 = bf16[32,1,49280]{2,1,0:T(2,128)(2,1)} reshape(bf16[32,2,24640]{2,1,0:T(2,128)(2,1)S(1)} %all-to-all-done) | data formatting | bytes 6307840
  233.5 3.1 %copy.45 = bf16[32,1,49280]{2,0,1:T(8,128)(2,1)S(1)} copy(bf16[32,1,49280]{2,1,0:T(2,128)(2,1)} %reshape.539) | data formatting | bytes 6307840
  236.7 0.0 copy-start.4
  236.7 0.2 slice.39
  236.9 0.1 reshape.481
  237.0 0.7 gather_fusion.4
  237.8 0.2 fusion.6
  237.9 0.1 add.197
  238.0 0.1 reduce_max.19
  238.1 0.2 fusion.19
  238.4 0.1 fusion.20
  238.4 0.5 add_subtract_fusion
  239.0 5.7 %reshape.484 = bf16[384,4096]{1,0:T(8,128)(2,1)} reshape(bf16[32,49152]{1,0:T(8,128)(2,1)S(1)} %slice.39) | data formatting | bytes 6291456 | tf_op jit(solution)/shard_map/reshape | solution.py:108
  244.7 3.4 %copy.41 = bf16[384,4096]{0,1:T(8,128)(2,1)S(1)} copy(bf16[384,4096]{1,0:T(8,128)(2,1)} %reshape.484) | data formatting | bytes 6291456 | tf_op jit(solution)/shard_map/reshape | solution.py:108
  248.1 0.1 select_reduce_fusion
  248.2 0.9 fusion.12
  249.2 0.7 copy.42
  (28 shorter events, 0.2 us)
Async XLA Ops:
  7.2 56.7 %copy-start = (s32[8192]{0:T(1024)S(1)}, s32[8192]{0:T(1024)}, u32[]{:S(2)}) copy-start(s32[8192]{0:T(1024)} %param.7) | copy-start | bytes 98308
  7.2 95.7 %all-gather.3.cloned.1.call-start = ((), (), s32[]{:S(2)}) async-start(), calls=%async_computation.1 | async-start | bytes 2359296 | tf_op jit(solution)/shard_map/all_gather | solution.py:47
  117.0 5.8 %copy-start.1 = (f32[384,32,128]{2,1,0:T(8,128)S(1)}, f32[384,32,128]{2,1,0:T(8,128)}, u32[]{:S(2)}) copy-start(f32[384,32,128]{2,1,0:T(8,128)} %get-tuple-element.24) | copy-start | bytes 18874372
  135.9 1.7 copy-start.2
  146.7 6.5 %copy-start.3 = (s32[8,16]{1,0:T(8,128)S(1)}, s32[8,16]{1,0:T(8,128)}, u32[]{:S(2)}) copy-start(s32[8,16]{1,0:T(8,128)} %param.8) | copy-start | bytes 1540
  146.7 70.4 %all-to-all-start = ((bf16[32,2,24640]{2,1,0:T(2,128)(2,1)}), bf16[32,2,24640]{2,1,0:T(2,128)(2,1)S(1)}, u32[]{:S(2)}, u32[]{:S(2)}) async-start(bf16[32,2,24640]{2,1,0:T(2,128)(2,1)} %reshape.538), calls=%async_computation | async-start | bytes 6324224 | tf_op jit(solution)/shard_map/all_to_all | solution.py:92
  236.7 1.5 copy-start.4
Sparse Core Ops, SparseCore 0:
  21.8 42.7 all-gather.2
where the time goes:
time: 257 us
  local copies, waits for them, and re-layouts  85.3 us (33%)
  waiting for transfers between devices  62 us (24%)
  blocking collectives  54.7 us (21%)
  matrix products  19.4 us (8%)
  other arithmetic  14.4 us (6%)
  between operations  14.4 us (6%)
  starting transfers between devices  6.57 us (3%)
    all_to_all x1, waiting for transfers between devices, body(): returned = lax.all_to_all(payload, BANK, 0, 0, tiled=True)  62 us
    all_gather x1, blocking collectives, gather_bank(): return lax.all_gather(value, 'z', axis=0, tiled=True)  28.2 us
    unnamed x18, local copies, waits for them, and re-layouts  27.9 us
    all_gather x2, blocking collectives, gather_bank(): value = lax.all_gather(value, 'y', axis=0, tiled=True)  26.5 us
    gather x1, local copies, waits for them, and re-layouts, body(): storage = passage_home[group_candidates].reshape(shards, entries)  23 us
    gather x1, local copies, waits for them, and re-layouts, body(): passage_tiles = passages[local_slot]  14.4 us
    dot_general x1, matrix products, body(): jnp.einsum('sid,sjd->sij', query_tiles, passage_tiles, preferred_element_...  11.3 us
    reshape x2, local copies, waits for them, and re-layouts, body(): bases = returned[:, :capacity * width].reshape(shards * capacity, width)  9.12 us
  transfers between devices with their start and end apart: 2, of which 1 were waited for; matrix products, arithmetic and copies ran while one was open for 17% of the time, Pallas kernels for 0%

commit v1 on v0

--- a/solution.py
+++ b/solution.py
@@ -44,7 +44,9 @@
 
 def gather_bank(value):
     value = lax.all_gather(value, "y", axis=0, tiled=True)
-    return lax.all_gather(value, "z", axis=0, tiled=True)
+    return jnp.concatenate(
+        lax.all_to_all(jnp.stack([value] * lax.axis_size("z")), "z", 0, 0), axis=0
+    )
 
 
 def body(queries, passages, passage_home, candidates, positive):

time: 257 us -> 248 us (0.965)
  blocking collectives: 54.7 us -> 25 us
  starting transfers between devices: 6.57 us -> 20.7 us
  between operations: 14.4 us -> 0.98 us
  waiting for transfers between devices: 62 us -> 73.8 us
  matrix products: 19.4 us -> 22.9 us
  local copies, waits for them, and re-layouts: 85.3 us -> 88.7 us
    all_gather x1 -> x0, blocking collectives: 28.2 us -> none  [gather_bank(): return lax.all_gather(value, 'z', axis=0, tiled=True)]
    all_to_all x0 -> x2, starting transfers between devices: none -> 15.7 us  [gather_bank(): lax.all_to_all(jnp.stack([value] * lax.axis_size('z')), 'z', 0, 0)]
    all_to_all x1, waiting for transfers between devices: 62 us -> 69.2 us  [body(): returned = lax.all_to_all(payload, BANK, 0, 0, tiled=True)]
    all_to_all x0 -> x2, waiting for transfers between devices: none -> 4.6 us  [gather_bank(): lax.all_to_all(jnp.stack([value] * lax.axis_size('z')), 'z', 0, 0)]
    dot_general x1, matrix products: 11.3 us -> 14.8 us  [body(): jnp.einsum('sid,sjd->sij', query_tiles, passage_tiles, preferred_element_...]
    unnamed x18 -> x19, local copies, waits for them, and re-layouts: 27.9 us -> 28.5 us
  transfers between devices with their start and end apart: 2 -> 3, of which waited for: 1 -> 2; matrix products, arithmetic and copies ran while one was open for 17% -> 17% of each run, Pallas kernels for 0% -> 0%
where the time goes in v1:
time: 248 us; the launch traced here: 247 us
  local copies, waits for them, and re-layouts  88.7 us (36%)
  waiting for transfers between devices  73.8 us (30%)
  blocking collectives  25 us (10%)
  matrix products  22.9 us (9%)
  starting transfers between devices  20.7 us (8%)
  other arithmetic  15.1 us (6%)
    all_to_all x1, waiting for transfers between devices, body(): returned = lax.all_to_all(payload, BANK, 0, 0, tiled=True)  69.2 us
    unnamed x19, local copies, waits for them, and re-layouts  28.5 us
    all_gather x2, blocking collectives, gather_bank(): value = lax.all_gather(value, 'y', axis=0, tiled=True)  25 us
    gather x1, local copies, waits for them, and re-layouts, body(): storage = passage_home[group_candidates].reshape(shards, entries)  23 us
    all_to_all x2, starting transfers between devices, gather_bank(): lax.all_to_all(jnp.stack([value] * lax.axis_size('z')), 'z', 0, 0)  15.7 us
    dot_general x1, matrix products, body(): jnp.einsum('sid,sjd->sij', query_tiles, passage_tiles, preferred_element_...  14.8 us
    gather x1, local copies, waits for them, and re-layouts, body(): passage_tiles = passages[local_slot]  14.4 us
    reshape x2, local copies, waits for them, and re-layouts, body(): bases = returned[:, :capacity * width].reshape(shards * capacity, width)  9.12 us
  transfers between devices with their start and end apart: 3, of which 2 were waited for; matrix products, arithmetic and copies ran while one was open for 17% of the time, Pallas kernels for 0%

profile of v1, /device:TPU:2, one launch (start us, length us, event | category | flops | bytes accessed | tf_op | source)
XLA Modules:
  0.0 247.1 jit_solution(7843358409571720024)
XLA Ops:
  0.6 0.7 copy.27
  1.4 0.8 pad_add_fusion
  2.1 12.5 %all_gather.7 = s32[32,17]{1,0:T(8,128)S(1)} all-gather(s32[8,17]{1,0:T(8,128)S(1)} %pad_add_fusion), channel_id=1, replica_groups=mesh['query'=8,'z'=8,'y'=4] {'y'}, dimensions={0}, use_global_device_ids=true | all-gather | bytes 2720 | tf_op jit(solution)/shard_map/all_gather | solution.py:46
  14.7 0.1 copy.28
  14.8 0.7 reshape.548
  15.5 8.5 %all-to-all-start.1 = ((s32[8,1,544]{2,1,0:T(1,128)}), s32[8,1,544]{2,1,0:T(1,128)S(1)}, u32[]{:S(2)}, u32[]{:S(2)}) async-start(s32[8,1,544]{2,1,0:T(1,128)} %reshape.548), calls=%async_computation.1 | async-start | bytes 40960 | tf_op jit(solution)/shard_map/all_to_all | solution.py:48
  23.9 12.5 %all_gather.6 = bf16[32,32,128]{2,1,0:T(8,128)(2,1)S(1)} all-gather(bf16[8,32,128]{2,1,0:T(8,128)(2,1)} %param.5), channel_id=1, replica_groups=mesh['query'=8,'z'=8,'y'=4] {'y'}, dimensions={0}, use_global_device_ids=true | all-gather | bytes 327680 | tf_op jit(solution)/shard_map/all_gather | solution.py:46
  36.4 1.7 stack.7
  38.1 7.2 %all-to-all-start = ((bf16[8,32,32,128]{3,2,1,0:T(8,128)(2,1)}), bf16[8,32,32,128]{3,2,1,0:T(8,128)(2,1)S(1)}, u32[]{:S(2)}, u32[]{:S(2)}) async-start(bf16[8,32,32,128]{3,2,1,0:T(8,128)(2,1)} %stack.7), calls=%async_computation | async-start | bytes 4194304 | tf_op jit(solution)/shard_map/all_to_all | solution.py:48
  45.4 0.1 add.181
  45.5 0.5 broadcast.449
  46.0 0.7 reduce.6
  46.7 0.1 reshape.549
  46.8 0.1 reshape.489
  46.9 0.1 copy.30
  47.0 0.1 reshape.499
  47.2 23.0 %gather_fusion = s32[4096]{0:T(1024)S(1)} fusion(s32[8192]{0:T(1024)S(1)} %copy-done, s32[4096]{0:T(1024)S(1)} %broadcast_clamp_fusion), kind=kCustom, calls=%fused_computation | custom fusion | bytes 49152 | tf_op jit(solution)/shard_map/gather | solution.py:65
  70.2 0.3 reduce_window_sum.22
  70.5 0.5 select_reduce_fusion.2
  71.0 0.1 copy.32
  71.1 0.1 reshape.491
  71.2 0.1 copy.31
  71.3 0.1 reduce_sum.81
  71.5 14.4 %gather_fusion.2 = bf16[384,128,128]{2,1,0:T(8,128)(2,1)} fusion(bf16[256,128,128]{2,1,0:T(8,128)(2,1)} %param.6, s32[1024]{0:T(1024)S(1)} %pad_clamp_fusion.2), kind=kCustom, calls=%fused_computation.2 | custom fusion | bytes 25167360 | tf_op jit(solution)/shard_map/gather | solution.py:76
  85.9 4.6 %all-to-all-done = bf16[8,32,32,128]{3,2,1,0:T(8,128)(2,1)S(1)} async-done(((bf16[8,32,32,128]{3,2,1,0:T(8,128)(2,1)}), bf16[8,32,32,128]{3,2,1,0:T(8,128)(2,1)S(1)}, u32[]{:S(2)}, u32[]{:S(2)}) %all-to-all-start) | async-done | bytes 2097184 | tf_op jit(solution)/shard_map/all_to_all | solution.py:48
  90.5 3.2 %gather_fusion.1 = bf16[384,32,128]{2,1,0:T(8,128)(2,1)} fusion(bf16[256,32,128]{2,1,0:T(8,128)(2,1)S(1)} %bitcast.64, s32[1024]{0:T(1024)S(1)} %pad_clamp_fusion.3), kind=kCustom, calls=%fused_computation.1 | custom fusion | bytes 6292992 | tf_op jit(solution)/shard_map/gather | solution.py:77
  93.7 14.8 %fusion.27 = (f32[384,32]{1,0:T(8,128)S(1)}, f32[384,32,128]{2,1,0:T(8,128)}) fusion(bf16[384,32,128]{2,1,0:T(8,128)(2,1)} %gather_fusion.1, bf16[384,128,128]{2,1,0:T(8,128)(2,1)} %gather_fusion.2), kind=kOutput, calls=%fused_computation.94 | convolution fusion | flops 404213760 | bytes 22069248 | tf_op jit(solution)/shard_map/sid,sjd->sij/dot_general | solution.py:78
  108.5 5.8 %fusion = f32[384,32]{1,0:T(8,128)S(1)} fusion(f32[384,32,128]{2,1,0:T(8,128)} %get-tuple-element.22, f32[384,32]{1,0:T(8,128)S(1)} %get-tuple-element.21), kind=kLoop, calls=%fused_computation.7 | loop fusion | flops 3133440 | bytes 6389760 | tf_op jit(solution)/shard_map/reduce_sum | solution.py:14
  114.4 7.1 %fusion.4 = bf16[384,32,128]{2,1,0:T(8,128)(2,1)S(1)} fusion(bf16[384,128,128]{2,1,0:T(8,128)(2,1)} %gather_fusion.2, f32[384,32,128]{2,1,0:T(8,128)S(1)} %copy-done.1, f32[384,32]{1,0:T(8,128)S(1)} %fusion, f32[384,32]{1,0:T(8,128)S(1)} %get-tuple-element.21), kind=kOutput, calls=%fused_computation.12 | convolution fusion | flops 408944640 | bytes 22118400 | tf_op jit(solution)/shard_map/sij,sjd->sid/dot_general | solution.py:82
  121.5 0.2 add_reduce_fusion
  121.7 2.8 %reshape.492 = bf16[32,49152]{1,0:T(8,128)(2,1)} reshape(bf16[384,32,128]{2,1,0:T(8,128)(2,1)S(1)} %fusion.4) | data formatting | bytes 6291456 | tf_op jit(solution)/shard_map/reshape | solution.py:88
  124.5 2.1 constant_dynamic-update-slice_fusion
  126.7 0.2 copy.33
  126.8 0.1 convert_element_type.52
  127.0 0.3 dynamic-update-slice.1
  127.3 0.3 dynamic-update-slice.2
  127.6 1.7 copy-done.2
  129.3 0.5 broadcast.450
  129.8 5.0 %reduce.7 = bf16[32,49280]{1,0:T(8,128)(2,1)S(1)} reduce(bf16[32,1,49280]{2,0,1:T(8,128)(2,1)} %bitcast.67, bf16[]{:T(256)} %broadcast.450), dimensions={1}, to_apply=%copy.34.reduce_sub_computation | reduce | bytes 6307842 | tf_op jit(solution)/shard_map/all_to_all | solution.py:94
  134.8 3.4 %reshape.550 = bf16[32,2,24640]{2,1,0:T(2,128)(2,1)} reshape(bf16[32,49280]{1,0:T(8,128)(2,1)S(1)} %reduce.7) | data formatting | bytes 6307840
  138.2 5.0 %all-to-all-start.2 = ((bf16[32,2,24640]{2,1,0:T(2,128)(2,1)}), bf16[32,2,24640]{2,1,0:T(2,128)(2,1)S(1)}, u32[]{:S(2)}, u32[]{:S(2)}) async-start(bf16[32,2,24640]{2,1,0:T(2,128)(2,1)} %reshape.550), calls=%async_computation.2 | async-start | bytes 6324224 | tf_op jit(solution)/shard_map/all_to_all | solution.py:94
  143.3 0.1 reshape.523
  143.4 1.1 gather_fusion.3
  144.6 0.1 reshape.522
  144.7 0.1 fusion.7
  144.7 0.2 reduce_window_sum.23
  144.9 0.2 select_reduce_fusion.3
  145.1 0.1 reduce_sum.90
  145.2 69.2 %all-to-all-done.2 = bf16[32,2,24640]{2,1,0:T(2,128)(2,1)S(1)} async-done(((bf16[32,2,24640]{2,1,0:T(2,128)(2,1)}), bf16[32,2,24640]{2,1,0:T(2,128)(2,1)S(1)}, u32[]{:S(2)}, u32[]{:S(2)}) %all-to-all-start.2) | async-done | bytes 3153952 | tf_op jit(solution)/shard_map/all_to_all | solution.py:94
  214.5 16.4 %reshape.551 = bf16[32,1,49280]{2,1,0:T(2,128)(2,1)} reshape(bf16[32,2,24640]{2,1,0:T(2,128)(2,1)S(1)} %all-to-all-done.2) | data formatting | bytes 6307840
  230.8 3.1 %copy.39 = bf16[32,1,49280]{2,0,1:T(8,128)(2,1)S(1)} copy(bf16[32,1,49280]{2,1,0:T(2,128)(2,1)} %reshape.551) | data formatting | bytes 6307840
  234.0 0.2 slice.39
  234.2 0.1 reshape.493
  234.3 0.7 gather_fusion.4
  235.0 0.2 fusion.6
  235.2 0.1 add.197
  235.3 0.1 reduce_max.19
  235.4 0.2 fusion.19
  235.7 0.5 add_subtract_fusion
  236.3 5.7 %reshape.496 = bf16[384,4096]{1,0:T(8,128)(2,1)} reshape(bf16[32,49152]{1,0:T(8,128)(2,1)S(1)} %slice.39) | data formatting | bytes 6291456 | tf_op jit(solution)/shard_map/reshape | solution.py:110
  242.0 3.4 %copy.35 = bf16[384,4096]{0,1:T(8,128)(2,1)S(1)} copy(bf16[384,4096]{1,0:T(8,128)(2,1)} %reshape.496) | data formatting | bytes 6291456 | tf_op jit(solution)/shard_map/reshape | solution.py:110
  245.4 0.1 select_reduce_fusion
  245.5 0.9 fusion.12
  246.4 0.7 copy.36
  (34 shorter events, 0.4 us)
Async XLA Ops:
  0.6 46.5 %copy-start = (s32[8192]{0:T(1024)S(1)}, s32[8192]{0:T(1024)}, u32[]{:S(2)}) copy-start(s32[8192]{0:T(1024)} %param.7) | copy-start | bytes 98308
  15.5 20.9 %all-to-all-start.1 = ((s32[8,1,544]{2,1,0:T(1,128)}), s32[8,1,544]{2,1,0:T(1,128)S(1)}, u32[]{:S(2)}, u32[]{:S(2)}) async-start(s32[8,1,544]{2,1,0:T(1,128)} %reshape.548), calls=%async_computation.1 | async-start | bytes 40960 | tf_op jit(solution)/shard_map/all_to_all | solution.py:48
  38.1 52.4 %all-to-all-start = ((bf16[8,32,32,128]{3,2,1,0:T(8,128)(2,1)}), bf16[8,32,32,128]{3,2,1,0:T(8,128)(2,1)S(1)}, u32[]{:S(2)}, u32[]{:S(2)}) async-start(bf16[8,32,32,128]{3,2,1,0:T(8,128)(2,1)} %stack.7), calls=%async_computation | async-start | bytes 4194304 | tf_op jit(solution)/shard_map/all_to_all | solution.py:48
  108.5 5.8 %copy-start.1 = (f32[384,32,128]{2,1,0:T(8,128)S(1)}, f32[384,32,128]{2,1,0:T(8,128)}, u32[]{:S(2)}) copy-start(f32[384,32,128]{2,1,0:T(8,128)} %get-tuple-element.22) | copy-start | bytes 18874372
  127.6 1.7 copy-start.2
  138.2 5.0 %copy-start.3 = (s32[8,16]{1,0:T(8,128)S(1)}, s32[8,16]{1,0:T(8,128)}, u32[]{:S(2)}) copy-start(s32[8,16]{1,0:T(8,128)} %param.8) | copy-start | bytes 1540
  138.2 76.2 %all-to-all-start.2 = ((bf16[32,2,24640]{2,1,0:T(2,128)(2,1)}), bf16[32,2,24640]{2,1,0:T(2,128)(2,1)S(1)}, u32[]{:S(2)}, u32[]{:S(2)}) async-start(bf16[32,2,24640]{2,1,0:T(2,128)(2,1)} %reshape.550), calls=%async_computation.2 | async-start | bytes 6324224 | tf_op jit(solution)/shard_map/all_to_all | solution.py:94
  234.0 1.5 copy-start.4
